TPU v7x, 256 devices: a whole 4x4x8 slice. The times are simulated.
256 devices in a mesh: seq: 64 (over x, z, core), ch: 4 (over y).
Axes of the slice: x: 4, y: 4, z: 8, core: 2. Of those that a mesh axis runs over, the one named last changes fastest.
Arguments:
- inputs: bfloat16 [8192, 4096], P('seq'), may hold values from -6 to 6
- norm_gain: float32 [4096], replicated, may hold values from 0.1 to 1.9
- in_weight: bfloat16 [4096, 3, 1024], P('seq', None, 'ch'), may hold values from -0.09375 to 0.09375
- short_filter: float32 [3, 3, 1024], P(None, None, 'ch'), may hold values from -4 to 4
- long_filter: float32 [8192, 1024], P('seq', 'ch'), may hold values from -2.2 to 2.2
- conv_bias: float32 [1024], P('ch'), may hold values from -4 to 4
- out_weight: bfloat16 [1024, 4096], P('ch', 'seq'), may hold values from -0.1875 to 0.1875
- out_grad: bfloat16 [8192, 4096], P('seq'), may hold values from -6 to 6
Outputs:
- block_out: bfloat16 [8192, 4096], P('seq', 'ch')
- in_grad: bfloat16 [8192, 4096], P('seq')
- filter_grad: float32 [8192, 1024], P('seq', 'ch')
All inputs are finite; a program needn't handle non-finite values.
Results may differ from a plain program's by a relative error of at most 0.013.
Values may be sent and summed in bfloat16 or wider, within the bound.
No kernel may reach another device: no remote copies, remote signals or barrier semaphores. Data moves between devices by JAX's collectives and lax.ppermute only.
A program may use at most 64 MiB of HBM per device.

v0:
```python
import math
import jax
import jax.numpy as jnp
from jax import lax
from jax.sharding import PartitionSpec as P

epsilon = 1e-05
highest = lax.Precision.HIGHEST


def passed_along(block, axis, distance):
    devices = range(lax.axis_size(axis))
    route = [(i - distance, i) for i in devices if i - distance in devices]
    return lax.ppermute(block, axis, route)


def to_columns(signals):
    return lax.all_to_all(signals, "seq", split_axis=1, concat_axis=2, tiled=True)


def to_rows(signals):
    return lax.all_to_all(signals, "seq", split_axis=2, concat_axis=1, tiled=True)


def turn_table(rows, cols, period, sign):
    turns = jnp.arange(rows, dtype=jnp.int32)[:, None] * jnp.arange(cols, dtype=jnp.int32)[None, :]
    phases = sign * 2.0 * math.pi / period * (turns % period).astype(jnp.float32)
    return (jnp.cos(phases), jnp.sin(phases))


def fft_sizes(seq_total):
    total = 2 * seq_total
    inner = 1
    while inner * inner < total:
        inner *= 2
    return (total // inner, inner)


def forward_dft(signals):
    count, chans, seq_total = signals.shape
    outer, inner = fft_sizes(seq_total)
    grid = signals.reshape(count, chans, outer // 2, inner)
    cos_out, sin_out = turn_table(outer, outer // 2, outer, 1.0)
    first_real = jnp.einsum("kn,ucnm->uckm", cos_out, grid, precision=highest)
    first_imag = -jnp.einsum("kn,ucnm->uckm", sin_out, grid, precision=highest)
    cos_tw, sin_tw = turn_table(outer, inner, outer * inner, 1.0)
    turned_real = first_real * cos_tw + first_imag * sin_tw
    turned_imag = first_imag * cos_tw - first_real * sin_tw
    cos_in, sin_in = turn_table(inner, inner, inner, 1.0)
    spec_real = jnp.einsum("uckm,mj->uckj", turned_real, cos_in, precision=highest) + jnp.einsum(
        "uckm,mj->uckj", turned_imag, sin_in, precision=highest
    )
    spec_imag = jnp.einsum("uckm,mj->uckj", turned_imag, cos_in, precision=highest) - jnp.einsum(
        "uckm,mj->uckj", turned_real, sin_in, precision=highest
    )
    return (spec_real, spec_imag)


def inverse_dft(spec_real, spec_imag):
    count, chans, outer, inner = spec_real.shape
    cos_in, sin_in = turn_table(inner, inner, inner, 1.0)
    back_real = jnp.einsum("uckj,jm->uckm", spec_real, cos_in, precision=highest) - jnp.einsum(
        "uckj,jm->uckm", spec_imag, sin_in, precision=highest
    )
    back_imag = jnp.einsum("uckj,jm->uckm", spec_imag, cos_in, precision=highest) + jnp.einsum(
        "uckj,jm->uckm", spec_real, sin_in, precision=highest
    )
    cos_tw, sin_tw = turn_table(outer, inner, outer * inner, 1.0)
    turned_real = back_real * cos_tw - back_imag * sin_tw
    turned_imag = back_imag * cos_tw + back_real * sin_tw
    cos_out, sin_out = turn_table(outer, outer // 2, outer, 1.0)
    grid = jnp.einsum("kn,uckm->ucnm", cos_out, turned_real, precision=highest) - jnp.einsum(
        "kn,uckm->ucnm", sin_out, turned_imag, precision=highest
    )
    return grid.reshape(count, chans, outer * inner // 2) / float(outer * inner)


def per_device(
    inputs, norm_gain, in_weight, short_filter, long_filter, conv_bias, out_weight, out_grad
):
    local_rows = inputs.shape[0]
    model_width = inputs.shape[1]
    slab_width = long_filter.shape[1]
    taps = short_filter.shape[1]
    wide_inputs = inputs.astype(jnp.float32)
    inv_rms = lax.rsqrt(jnp.mean(wide_inputs * wide_inputs, axis=1, keepdims=True) + epsilon)
    normed = (wide_inputs * inv_rms * norm_gain).astype(jnp.bfloat16)
    in_panel, out_panel = (
        lax.all_gather(in_weight, "seq", axis=0, tiled=True),
        lax.all_gather(out_weight, "seq", axis=1, tiled=True),
    )
    in_flat = in_panel.reshape(model_width, 3 * slab_width)
    projected = jnp.dot(normed, in_flat, preferred_element_type=jnp.float32)
    projected = projected.astype(jnp.bfloat16).reshape(local_rows, 3, slab_width)
    upper_rim = passed_along(projected[local_rows - (taps - 1) :], "seq", 1)
    extended = jnp.concatenate([upper_rim, projected], 0).astype(jnp.float32)
    mixed = jnp.zeros((local_rows, 3, slab_width), jnp.float32)
    for offset in range(taps):
        begin = taps - 1 - offset
        mixed = mixed + short_filter[:, offset, :][None] * extended[begin : begin + local_rows]
    query_br = mixed[:, 0]
    key_br = mixed[:, 1]
    value_br = mixed[:, 2]
    product = key_br * value_br
    gate_grad = jnp.dot(out_grad, out_panel.T, preferred_element_type=jnp.float32)
    carried = gate_grad * query_br
    columns = to_columns(jnp.stack([product, long_filter, carried]).transpose(0, 2, 1))
    all_real, all_imag = forward_dft(columns)
    sig_real, filt_real, grad_real = (all_real[0], all_real[1], all_real[2])
    sig_imag, filt_imag, grad_imag = (all_imag[0], all_imag[1], all_imag[2])
    conv_real = sig_real * filt_real - sig_imag * filt_imag
    conv_imag = sig_real * filt_imag + sig_imag * filt_real
    back_real = grad_real * filt_real + grad_imag * filt_imag
    back_imag = grad_imag * filt_real - grad_real * filt_imag
    pair_real = grad_real * sig_real + grad_imag * sig_imag
    pair_imag = grad_imag * sig_real - grad_real * sig_imag
    outs = inverse_dft(
        jnp.stack([conv_real, back_real, pair_real]), jnp.stack([conv_imag, back_imag, pair_imag])
    )
    returned = to_rows(outs).transpose(0, 2, 1)
    conv_out = returned[0]
    back_conv = returned[1]
    filter_grad = returned[2] * float(local_rows * lax.axis_size("seq")) ** (-0.5)
    biased = conv_out + conv_bias * product
    gated = (query_br * biased).astype(jnp.bfloat16)
    partial_out = jnp.dot(gated, out_panel, preferred_element_type=jnp.float32)
    summed = lax.psum_scatter(
        partial_out.astype(jnp.bfloat16), "ch", scatter_dimension=1, tiled=True
    ).astype(jnp.float32)
    share = summed.shape[1]
    residual = lax.dynamic_slice_in_dim(wide_inputs, lax.axis_index("ch") * share, share, 1)
    block_out = (residual + summed).astype(jnp.bfloat16)
    source_grad = back_conv + conv_bias * carried
    mixed_grad = jnp.stack([gate_grad * biased, source_grad * value_br, source_grad * key_br], 1)
    lower_rim = passed_along(mixed_grad[: taps - 1], "seq", -1)
    extended_back = jnp.concatenate([mixed_grad, lower_rim], 0)
    proj_grad = jnp.zeros((local_rows, 3, slab_width), jnp.float32)
    for offset in range(taps):
        proj_grad = (
            proj_grad
            + short_filter[:, offset, :][None] * extended_back[offset : offset + local_rows]
        )
    proj_grad = proj_grad.astype(jnp.bfloat16).reshape(local_rows, 3 * slab_width)
    partial_grad = jnp.dot(proj_grad, in_flat.T, preferred_element_type=jnp.float32)
    norm_grad = lax.psum(partial_grad, "ch")
    weighted = norm_grad * norm_gain
    inner_term = jnp.mean(weighted * wide_inputs, axis=1, keepdims=True)
    in_grad = (
        out_grad.astype(jnp.float32) + weighted * inv_rms - wide_inputs * inv_rms**3 * inner_term
    ).astype(jnp.bfloat16)
    return (block_out, in_grad, filter_grad)


def solution(mesh):
    return jax.shard_map(
        per_device,
        mesh=mesh,
        in_specs=(
            P("seq", None),
            P(),
            P("seq", None, "ch"),
            P(None, None, "ch"),
            P("seq", "ch"),
            P("ch"),
            P("ch", "seq"),
            P("seq", None),
        ),
        out_specs=(P("seq", "ch"), P("seq", None), P("seq", "ch")),
        check_vma=False,
    )
```

profile of v0, /device:TPU:1, one launch (start us, length us, event | category | flops | bytes accessed | tf_op | source)
XLA Modules:
  0.0 393.4 jit_solution(6677568835043596494)
XLA Ops:
  11.6 83.9 %all-gather.3.cloned.1.call-done = bf16[4096,3,256]{2,0,1:T(8,128)(2,1)} async-done(((bf16[64,3,256]{2,0,1:T(8,128)(2,1)}), bf16[4096,3,256]{2,0,1:T(8,128)(2,1)}) %all-gather.3.cloned.1.call-update) | async-done | bytes 6291472 | tf_op jit(solution)/shard_map/all_gather | solution.py:89
  95.5 8.7 %copy.46 = bf16[4096,3,256]{0,2,1:T(8,128)(2,1)} copy(bf16[4096,3,256]{2,0,1:T(8,128)(2,1)} %all-gather.3.cloned.1.call-done) | data formatting | bytes 12582912 | tf_op jit(solution)/shard_map/all_gather | solution.py:89
  104.2 5.1 %convolution_convert_fusion.1 = bf16[128,768]{1,0:T(8,128)(2,1)S(1)} fusion(bf16[4096,768]{0,1:T(8,128)(2,1)} %bitcast.127, bf16[128,4096]{1,0:T(8,128)(2,1)S(1)} %copy-done, f32[4096]{0:T(1024)S(1)} %copy-done.9, f32[128]{0:T(128)S(1)} %get-tuple-element.19), kind=kOutput, calls=%fused_computation.16 | convolution fusion | flops 807501824 | bytes 7553536 | tf_op jit(solution)/shard_map/dot_general | solution.py:93
  109.3 2.7 collective-permute-start
  112.1 60.2 %all-gather.5.cloned.1.call-done = bf16[256,4096]{0,1:T(8,128)(2,1)} async-done(((bf16[256,64]{0,1:T(8,128)(2,1)}), bf16[256,4096]{0,1:T(8,128)(2,1)}) %all-gather.5.cloned.1.call-update) | async-done | bytes 2097168 | tf_op jit(solution)/shard_map/all_gather | solution.py:90
  172.3 2.0 fusion.143
  176.4 6.6 %all-to-all-start = ((f32[3,256,128]{2,0,1:T(4,128)}), f32[3,256,128]{2,0,1:T(4,128)S(1)}, u32[]{:S(2)}, u32[]{:S(2)}) async-start(f32[3,256,128]{2,0,1:T(4,128)} %copy.50), calls=%async_computation | async-start | bytes 1048576 | tf_op jit(solution)/shard_map/all_to_all | solution.py:18
  183.9 16.3 %all-to-all-done = f32[3,256,128]{2,0,1:T(4,128)S(1)} async-done(((f32[3,256,128]{2,0,1:T(4,128)}), f32[3,256,128]{2,0,1:T(4,128)S(1)}, u32[]{:S(2)}, u32[]{:S(2)}) %all-to-all-start) | async-done | bytes 393248 | tf_op jit(solution)/shard_map/all_to_all | solution.py:18
  217.0 8.6 %copy.85 = f32[3,4,64,128]{1,0,3,2:T(4,128)} copy(f32[3,4,64,128]{3,2,1,0:T(8,128)S(1)} %fusion.2) | data formatting | bytes 786432 | tf_op jit(solution)/shard_map/div | solution.py:75
  225.6 16.0 %reshape.105 = f32[64,1,1536]{2,1,0:T(1,128)S(1)} reshape(f32[8192,3,4]{2,1,0:T(4,128)} %bitcast.125) | data formatting | bytes 786432
  241.6 20.6 %all_to_all.33 = f32[64,1,1536]{2,1,0:T(1,128)S(1)} all-to-all(f32[64,1,1536]{2,1,0:T(1,128)S(1)} %reshape.105), channel_id=1, replica_groups=mesh['seq'=64,'ch'=4] {'seq'}, dimensions={0} | all-to-all | bytes 786432 | tf_op jit(solution)/shard_map/all_to_all | solution.py:22
  264.4 11.6 %reshape.106 = f32[8192,3,4]{2,1,0:T(4,128)} reshape(f32[64,1536]{1,0:T(8,128)S(1)} %reduce) | data formatting | bytes 786432
  275.9 10.1 %copy.86 = f32[3,4,64,128]{3,2,1,0:T(8,128)} copy(f32[3,4,64,128]{1,0,3,2:T(4,128)} %bitcast.126) | data formatting | bytes 786432 | tf_op jit(solution)/shard_map/all_to_all | solution.py:22
  286.0 2.2 copy.67
  288.1 1.9 copy.68
  290.0 1.8 fusion.37
  295.7 2.6 collective-permute-start.1
  298.3 2.4 collective-permute-done.1
  300.7 6.4 %convolution_bitcast_fusion = f32[128,4096]{1,0:T(8,128)} fusion(bf16[4096,3,256]{2,0,1:T(8,128)(2,1)} %all-gather.3.cloned.1.call-done, f32[130,3,256]{2,0,1:T(8,128)S(1)} %pad_maximum_fusion.6, f32[3,256]{1,0:T(4,128)S(1)} %get-tuple-element.20, f32[3,256]{1,0:T(4,128)S(1)} %get-tuple-element.21, f32[3,256]{1,0:T(4,128)S(1)} %bitcast.136, ...), kind=kOutput, calls=%fused_computation | convolution fusion | flops 806092800 | bytes 9580544 | tf_op jit(solution)/shard_map/dot_general | solution.py:144
  310.3 5.3 %reduce-scatter.2.cloned.1.call-done = bf16[128,1024]{1,0:T(8,128)(2,1)} async-done(((bf16[128,4096]{1,0:T(8,128)(2,1)}), bf16[128,1024]{1,0:T(8,128)(2,1)}) %reduce-scatter.2.cloned.1.call-update) | async-done | bytes 262160 | tf_op jit(solution)/shard_map/reduce_scatter | solution.py:127
  315.6 1.9 add_convert_fusion
  317.5 65.3 %all-reduce.2.cloned.1.call-done = f32[128,4096]{1,0:T(8,128)} async-done(((f32[128,4096]{1,0:T(8,128)}), f32[128,4096]{1,0:T(8,128)}) %all-reduce.2.cloned.1.call-update) | async-done | bytes 2097168 | tf_op jit(solution)/shard_map/psum | solution.py:145
  382.8 2.1 multiply_reduce_fusion
  385.0 1.9 subtract_convert_fusion
  (81 shorter events, 33.1 us)
Async XLA Ops:
  7.2 88.3 %all-gather.3.cloned.1.call-start = ((), (), s32[]{:S(2)}) async-start(), calls=%async_computation.3 | async-start | bytes 6389760 | tf_op jit(solution)/shard_map/all_gather | solution.py:89
  7.9 164.4 %all-gather.5.cloned.1.call-start = ((), (), s32[]{:S(2)}) async-start(), calls=%async_computation.4 | async-start | bytes 2129920 | tf_op jit(solution)/shard_map/all_gather | solution.py:90
  11.6 92.6 %copy-start.13 = (f32[128]{0:T(128)}, f32[128]{0:T(128)S(1)}, u32[]{:S(2)}) copy-start(f32[128]{0:T(128)S(1)} %get-tuple-element.19) | copy-start | bytes 1540
  11.6 92.6 %copy-start = (bf16[128,4096]{1,0:T(8,128)(2,1)S(1)}, bf16[128,4096]{1,0:T(8,128)(2,1)}, u32[]{:S(2)}) copy-start(bf16[128,4096]{1,0:T(8,128)(2,1)} %param.8) | copy-start | bytes 3145732
  11.6 92.6 %copy-start.9 = (f32[4096]{0:T(1024)S(1)}, f32[4096]{0:T(1024)}, u32[]{:S(2)}) copy-start(f32[4096]{0:T(1024)} %param.9) | copy-start | bytes 49156
  104.2 68.1 %copy-start.3 = (bf16[128,4096]{1,0:T(8,128)(2,1)S(1)}, bf16[128,4096]{1,0:T(8,128)(2,1)}, u32[]{:S(2)}) copy-start(bf16[128,4096]{1,0:T(8,128)(2,1)} %param.15) | copy-start | bytes 3145732
  109.3 65.4 %collective-permute-start = (bf16[2,3,256]{2,0,1:T(2,128)(2,1)S(1)}, bf16[2,3,256]{2,0,1:T(2,128)(2,1)S(1)}, u32[]{:S(2)}, u32[]{:S(2)}) collective-permute-start(bf16[2,3,256]{2,0,1:T(2,128)(2,1)S(1)} %bitcast.138), channel_id=1, source_target_pairs={{0,4},{4,8},{8,12},{12,16},{16,20},{20,24},{24,28},{28,32},{32,36}... | collective-permute-start | bytes 9224 | tf_op jit(solution)/shard_map/ppermute | solution.py:14
  174.4 1.0 copy-start.7
  174.4 1.0 copy-start.8
  176.4 23.9 %all-to-all-start = ((f32[3,256,128]{2,0,1:T(4,128)}), f32[3,256,128]{2,0,1:T(4,128)S(1)}, u32[]{:S(2)}, u32[]{:S(2)}) async-start(f32[3,256,128]{2,0,1:T(4,128)} %copy.50), calls=%async_computation | async-start | bytes 1048576 | tf_op jit(solution)/shard_map/all_to_all | solution.py:18
  183.0 132.6 %reduce-scatter.2.cloned.1.call-start = ((), (), s32[]{:S(2)}) async-start(), calls=%async_computation.5 | async-start | bytes 1310720 | tf_op jit(solution)/shard_map/reduce_scatter | solution.py:127
  275.9 14.1 %copy-start.11 = (f32[256]{0:T(256)S(1)}, f32[256]{0:T(256)}, u32[]{:S(2)}) copy-start(f32[256]{0:T(256)} %param.13) | copy-start | bytes 3076
  286.0 5.9 %copy-start.1 = (bf16[256,4096]{0,1:T(8,128)(2,1)S(1)}, bf16[256,4096]{0,1:T(8,128)(2,1)}, u32[]{:S(2)}) copy-start(bf16[256,4096]{0,1:T(8,128)(2,1)} %all-gather.5.cloned.1.call-done) | copy-start | bytes 6291460
  293.6 7.0 %copy-start.5 = (f32[128,1,256]{2,0,1:T(8,128)S(1)}, f32[128,1,256]{2,0,1:T(8,128)}, u32[]{:S(2)}) copy-start(f32[128,1,256]{2,0,1:T(8,128)} %get-tuple-element.5) | copy-start | bytes 393220
  293.6 7.0 %copy-start.6 = (f32[128,1,256]{2,0,1:T(8,128)S(1)}, f32[128,1,256]{2,0,1:T(8,128)}, u32[]{:S(2)}) copy-start(f32[128,1,256]{2,0,1:T(8,128)} %get-tuple-element.13) | copy-start | bytes 393220
  293.7 89.1 %all-reduce.2.cloned.1.call-start = ((), (), s32[]{:S(2)}) async-start(), calls=%async_computation.6 | async-start | bytes 4194304 | tf_op jit(solution)/shard_map/psum | solution.py:145
  295.7 4.9 %collective-permute-start.1 = (f32[2,3,256]{2,0,1:T(2,128)S(1)}, f32[2,3,256]{2,0,1:T(2,128)S(1)}, u32[]{:S(2)}, u32[]{:S(2)}) collective-permute-start(f32[2,3,256]{2,0,1:T(2,128)S(1)} %slice.110), channel_id=1, source_target_pairs={{4,0},{8,4},{12,8},{16,12},{20,16},{24,20},{28,24},{32,28},{36,32}... | collective-permute-start | bytes 18440 | tf_op jit(solution)/shard_map/ppermute | solution.py:14
  307.1 75.6 %copy-start.10 = (f32[4096]{0:T(1024)S(1)}, f32[4096]{0:T(1024)}, u32[]{:S(2)}) copy-start(f32[4096]{0:T(1024)} %param.9) | copy-start | bytes 49156
  310.3 74.6 %copy-start.4 = (bf16[128,4096]{1,0:T(8,128)(2,1)S(1)}, bf16[128,4096]{1,0:T(8,128)(2,1)}, u32[]{:S(2)}) copy-start(bf16[128,4096]{1,0:T(8,128)(2,1)} %param.15) | copy-start | bytes 3145732
  310.3 74.6 %copy-start.12 = (f32[128]{0:T(128)S(1)}, f32[128]{0:T(128)}, u32[]{:S(2)}) copy-start(f32[128]{0:T(128)} %get-tuple-element.18) | copy-start | bytes 1540
  310.3 74.6 %copy-start.14 = (f32[128]{0:T(128)S(1)}, f32[128]{0:T(128)}, u32[]{:S(2)}) copy-start(f32[128]{0:T(128)} %copy-done.13) | copy-start | bytes 1540
  382.8 2.2 copy-start.2
Sparse Core Ops, SparseCore 0:
  10.8 84.6 all-gather.2
  98.3 74.0 all-gather.4
  293.8 21.7 reduce-scatter.1
  317.8 64.9 all-reduce.1
where the time goes:
time: 395 us; the launch traced here: 393 us
  waiting for transfers between devices  235 us (59%)
  local copies, waits for them, and re-layouts  62.4 us (16%)
  matrix products  31.7 us (8%)
  blocking collectives  20.6 us (5%)
  other arithmetic  17.5 us (4%)
  between operations  14.1 us (4%)
  starting transfers between devices  12.2 us (3%)
    all_gather x1, waiting for transfers between devices, per_device(): lax.all_gather(in_weight, 'seq', axis=0, tiled=True)  83.9 us
    psum x1, waiting for transfers between devices, per_device(): norm_grad = lax.psum(partial_grad, 'ch')  65.3 us
    all_gather x1, waiting for transfers between devices, per_device(): lax.all_gather(out_weight, 'seq', axis=1, tiled=True)  60.2 us
    unnamed x34, local copies, waits for them, and re-layouts  28.1 us
    all_to_all x1, blocking collectives, to_rows(): lax.all_to_all(signals, 'seq', split_axis=2, concat_axis=1, tiled=True)  20.6 us
    all_to_all x1, waiting for transfers between devices, to_columns(): lax.all_to_all(signals, 'seq', split_axis=1, concat_axis=2, tiled=True)  16.3 us
    all_to_all x4, local copies, waits for them, and re-layouts, to_rows(): lax.all_to_all(signals, 'seq', split_axis=2, concat_axis=1, tiled=True)  14.6 us
    all_gather x1, local copies, waits for them, and re-layouts, per_device(): lax.all_gather(in_weight, 'seq', axis=0, tiled=True)  8.7 us
  transfers between devices with their start and end apart: 7, of which 6 were waited for; matrix products, arithmetic and copies ran while one was open for 8% of the time, Pallas kernels for 0%

commit v1 on v0

--- a/solution.py
+++ b/solution.py
@@ -142,7 +142,11 @@
         )
     proj_grad = proj_grad.astype(jnp.bfloat16).reshape(local_rows, 3 * slab_width)
     partial_grad = jnp.dot(proj_grad, in_flat.T, preferred_element_type=jnp.float32)
-    norm_grad = lax.psum(partial_grad, "ch")
+    norm_grad = partial_grad
+    for hop in (1, 2):
+        norm_grad = norm_grad + lax.ppermute(
+            norm_grad, "ch", [(dev, dev ^ hop) for dev in range(4)]
+        )
     weighted = norm_grad * norm_gain
     inner_term = jnp.mean(weighted * wide_inputs, axis=1, keepdims=True)
     in_grad = (

time: 395 us -> 416 us (1.053)
  waiting for transfers between devices: 235 us -> 258 us
  local copies, waits for them, and re-layouts: 62.4 us -> 58 us
    ppermute x0 -> x2, waiting for transfers between devices: none -> 93.3 us  [per_device(): lax.ppermute(norm_grad, 'ch', [(dev, dev ^ hop) for dev in range(4)])]
    psum x1 -> x0, waiting for transfers between devices: 65.3 us -> none  [per_device(): norm_grad = lax.psum(partial_grad, 'ch')]
    reduce_scatter x1, waiting for transfers between devices: 5.28 us -> 0.01 us  [per_device(): lax.psum_scatter(partial_out.astype(jnp.bfloat16), 'ch', scatter_dimensio...]
    all_to_all x4, local copies, waits for them, and re-layouts: 14.6 us -> 10.3 us  [to_rows(): lax.all_to_all(signals, 'seq', split_axis=2, concat_axis=1, tiled=True)]
    unnamed x34 -> x28, local copies, waits for them, and re-layouts: 28.1 us -> 28 us
  transfers between devices with their start and end apart: 7 -> 8, of which waited for: 6 -> 6; matrix products, arithmetic and copies ran while one was open for 8% -> 7% of each run, Pallas kernels for 0% -> 0%
where the time goes in v1:
time: 416 us; the launch traced here: 415 us
  waiting for transfers between devices  258 us (62%)
  local copies, waits for them, and re-layouts  58 us (14%)
  matrix products  30.4 us (7%)
  blocking collectives  20.6 us (5%)
  other arithmetic  17.1 us (4%)
  starting transfers between devices  16.1 us (4%)
  between operations  14.2 us (3%)
    ppermute x2, waiting for transfers between devices, per_device(): lax.ppermute(norm_grad, 'ch', [(dev, dev ^ hop) for dev in range(4)])  93.3 us
    all_gather x1, waiting for transfers between devices, per_device(): lax.all_gather(in_weight, 'seq', axis=0, tiled=True)  84.4 us
    all_gather x1, waiting for transfers between devices, per_device(): lax.all_gather(out_weight, 'seq', axis=1, tiled=True)  60.2 us
    unnamed x28, local copies, waits for them, and re-layouts  28 us
    all_to_all x1, blocking collectives, to_rows(): lax.all_to_all(signals, 'seq', split_axis=2, concat_axis=1, tiled=True)  20.6 us
    all_to_all x1, waiting for transfers between devices, to_columns(): lax.all_to_all(signals, 'seq', split_axis=1, concat_axis=2, tiled=True)  16.3 us
    all_to_all x4, local copies, waits for them, and re-layouts, to_rows(): lax.all_to_all(signals, 'seq', split_axis=2, concat_axis=1, tiled=True)  10.3 us
    all_gather x1, local copies, waits for them, and re-layouts, per_device(): lax.all_gather(in_weight, 'seq', axis=0, tiled=True)  8.71 us
  transfers between devices with their start and end apart: 8, of which 6 were waited for; matrix products, arithmetic and copies ran while one was open for 7% of the time, Pallas kernels for 0%

profile of v1, /device:TPU:1, one launch (start us, length us, event | category | flops | bytes accessed | tf_op | source)
XLA Modules:
  0.0 414.7 jit_solution(11541212020376695205)
XLA Ops:
  11.1 84.4 %all-gather.3.cloned.1.call-done = bf16[4096,3,256]{2,0,1:T(8,128)(2,1)} async-done(((bf16[64,3,256]{2,0,1:T(8,128)(2,1)}), bf16[4096,3,256]{2,0,1:T(8,128)(2,1)}) %all-gather.3.cloned.1.call-update) | async-done | bytes 6291472 | tf_op jit(solution)/shard_map/all_gather | solution.py:89
  95.5 8.7 %copy.46 = bf16[4096,3,256]{0,2,1:T(8,128)(2,1)} copy(bf16[4096,3,256]{2,0,1:T(8,128)(2,1)} %all-gather.3.cloned.1.call-done) | data formatting | bytes 12582912 | tf_op jit(solution)/shard_map/all_gather | solution.py:89
  104.2 5.1 %convolution_convert_fusion.1 = bf16[128,768]{1,0:T(8,128)(2,1)S(1)} fusion(bf16[4096,768]{0,1:T(8,128)(2,1)} %bitcast.127, bf16[128,4096]{1,0:T(8,128)(2,1)S(1)} %copy-done, f32[4096]{0:T(1024)S(1)} %copy-done.7, f32[128]{0:T(128)S(1)} %get-tuple-element.19), kind=kOutput, calls=%fused_computation.17 | convolution fusion | flops 807501824 | bytes 7553536 | tf_op jit(solution)/shard_map/dot_general | solution.py:93
  109.4 2.7 collective-permute-start
  112.1 60.2 %all-gather.5.cloned.1.call-done = bf16[256,4096]{0,1:T(8,128)(2,1)} async-done(((bf16[256,64]{0,1:T(8,128)(2,1)}), bf16[256,4096]{0,1:T(8,128)(2,1)}) %all-gather.5.cloned.1.call-update) | async-done | bytes 2097168 | tf_op jit(solution)/shard_map/all_gather | solution.py:90
  172.3 2.0 fusion.143
  176.3 6.6 %all-to-all-start = ((f32[3,256,128]{2,0,1:T(4,128)}), f32[3,256,128]{2,0,1:T(4,128)S(1)}, u32[]{:S(2)}, u32[]{:S(2)}) async-start(f32[3,256,128]{2,0,1:T(4,128)} %copy.50), calls=%async_computation | async-start | bytes 1048576 | tf_op jit(solution)/shard_map/all_to_all | solution.py:18
  183.9 16.3 %all-to-all-done = f32[3,256,128]{2,0,1:T(4,128)S(1)} async-done(((f32[3,256,128]{2,0,1:T(4,128)}), f32[3,256,128]{2,0,1:T(4,128)S(1)}, u32[]{:S(2)}, u32[]{:S(2)}) %all-to-all-start) | async-done | bytes 393248 | tf_op jit(solution)/shard_map/all_to_all | solution.py:18
  216.9 8.7 %copy.85 = f32[3,4,64,128]{1,0,3,2:T(4,128)} copy(f32[3,4,64,128]{3,2,1,0:T(8,128)S(1)} %fusion.2) | data formatting | bytes 786432 | tf_op jit(solution)/shard_map/div | solution.py:75
  225.5 16.0 %reshape.105 = f32[64,1,1536]{2,1,0:T(1,128)S(1)} reshape(f32[8192,3,4]{2,1,0:T(4,128)} %bitcast.125) | data formatting | bytes 786432
  241.6 20.6 %all_to_all.33 = f32[64,1,1536]{2,1,0:T(1,128)S(1)} all-to-all(f32[64,1,1536]{2,1,0:T(1,128)S(1)} %reshape.105), channel_id=1, replica_groups=mesh['seq'=64,'ch'=4] {'seq'}, dimensions={0} | all-to-all | bytes 786432 | tf_op jit(solution)/shard_map/all_to_all | solution.py:22
  264.3 11.6 %reshape.106 = f32[8192,3,4]{2,1,0:T(4,128)} reshape(f32[64,1536]{1,0:T(8,128)S(1)} %reduce) | data formatting | bytes 786432
  275.9 9.4 %copy.86 = f32[3,4,64,128]{3,2,1,0:T(8,128)S(1)} copy(f32[3,4,64,128]{1,0,3,2:T(4,128)} %bitcast.126) | data formatting | bytes 786432 | tf_op jit(solution)/shard_map/all_to_all | solution.py:22
  285.9 2.3 collective-permute-start.1
  288.2 2.6 collective-permute-done.1
  290.9 5.1 %convolution_bitcast_fusion = f32[128,4096]{1,0:T(8,128)S(1)} fusion(bf16[4096,3,256]{2,0,1:T(8,128)(2,1)} %all-gather.3.cloned.1.call-done, f32[130,3,256]{2,0,1:T(8,128)S(1)} %pad_maximum_fusion.6, f32[3,256]{1,0:T(4,128)S(1)} %get-tuple-element.20, f32[3,256]{1,0:T(4,128)S(1)} %get-tuple-element.21, f32[3,256]{1,0:T(4,128)S(1)} %bitcast.136, ...), kind=kOutput, calls=%fused_computation | convolution fusion | flops 806092800 | bytes 9580544 | tf_op jit(solution)/shard_map/dot_general | solution.py:144
  297.3 1.8 convolution_convert_fusion
  299.1 51.8 %collective-permute-done.2 = f32[128,4096]{1,0:T(8,128)} collective-permute-done((f32[128,4096]{1,0:T(8,128)S(1)}, f32[128,4096]{1,0:T(8,128)}, u32[]{:S(2)}, u32[]{:S(2)}) %collective-permute-start.2) | collective-permute-done | bytes 2097184 | tf_op jit(solution)/shard_map/ppermute | solution.py:147
  350.9 2.4 add.156
  353.4 2.8 collective-permute-start.3
  359.3 1.9 add_convert_fusion
  361.2 41.4 %collective-permute-done.3 = f32[128,4096]{1,0:T(8,128)} collective-permute-done((f32[128,4096]{1,0:T(8,128)S(1)}, f32[128,4096]{1,0:T(8,128)}, u32[]{:S(2)}, u32[]{:S(2)}) %collective-permute-start.3) | collective-permute-done | bytes 2097184 | tf_op jit(solution)/shard_map/ppermute | solution.py:147
  402.6 2.0 multiply_reduce_fusion
  404.6 3.5 subtract_convert_fusion
  (77 shorter events, 30.3 us)
Async XLA Ops:
  7.2 88.3 %all-gather.3.cloned.1.call-start = ((), (), s32[]{:S(2)}) async-start(), calls=%async_computation.3 | async-start | bytes 6389760 | tf_op jit(solution)/shard_map/all_gather | solution.py:89
  7.9 164.4 %all-gather.5.cloned.1.call-start = ((), (), s32[]{:S(2)}) async-start(), calls=%async_computation.4 | async-start | bytes 2129920 | tf_op jit(solution)/shard_map/all_gather | solution.py:90
  11.0 93.2 %copy-start.10 = (f32[128]{0:T(128)}, f32[128]{0:T(128)S(1)}, u32[]{:S(2)}) copy-start(f32[128]{0:T(128)S(1)} %get-tuple-element.19) | copy-start | bytes 1540
  11.0 93.2 %copy-start = (bf16[128,4096]{1,0:T(8,128)(2,1)S(1)}, bf16[128,4096]{1,0:T(8,128)(2,1)}, u32[]{:S(2)}) copy-start(bf16[128,4096]{1,0:T(8,128)(2,1)} %param.8) | copy-start | bytes 3145732
  11.1 93.2 %copy-start.7 = (f32[4096]{0:T(1024)S(1)}, f32[4096]{0:T(1024)}, u32[]{:S(2)}) copy-start(f32[4096]{0:T(1024)} %param.9) | copy-start | bytes 49156
  104.2 68.1 %copy-start.3 = (bf16[128,4096]{1,0:T(8,128)(2,1)S(1)}, bf16[128,4096]{1,0:T(8,128)(2,1)}, u32[]{:S(2)}) copy-start(bf16[128,4096]{1,0:T(8,128)(2,1)} %param.15) | copy-start | bytes 3145732
  109.4 65.4 %collective-permute-start = (bf16[2,3,256]{2,0,1:T(2,128)(2,1)S(1)}, bf16[2,3,256]{2,0,1:T(2,128)(2,1)S(1)}, u32[]{:S(2)}, u32[]{:S(2)}) collective-permute-start(bf16[2,3,256]{2,0,1:T(2,128)(2,1)S(1)} %bitcast.138), channel_id=1, source_target_pairs={{0,4},{4,8},{8,12},{12,16},{16,20},{20,24},{24,28},{28,32},{32,36}... | collective-permute-start | bytes 9224 | tf_op jit(solution)/shard_map/ppermute | solution.py:14
  174.4 0.9 copy-start.6
  176.3 23.9 %all-to-all-start = ((f32[3,256,128]{2,0,1:T(4,128)}), f32[3,256,128]{2,0,1:T(4,128)S(1)}, u32[]{:S(2)}, u32[]{:S(2)}) async-start(f32[3,256,128]{2,0,1:T(4,128)} %copy.50), calls=%async_computation | async-start | bytes 1048576 | tf_op jit(solution)/shard_map/all_to_all | solution.py:18
  182.9 176.3 %reduce-scatter.2.cloned.1.call-start = ((), (), s32[]{:S(2)}) async-start(), calls=%async_computation.5 | async-start | bytes 1310720 | tf_op jit(solution)/shard_map/reduce_scatter | solution.py:127
  275.9 9.8 %copy-start.9 = (f32[256]{0:T(256)S(1)}, f32[256]{0:T(256)}, u32[]{:S(2)}) copy-start(f32[256]{0:T(256)} %param.13) | copy-start | bytes 3076
  285.7 5.1 %copy-start.5 = (f32[3,256,128]{1,2,0:T(8,128)}, f32[3,256,128]{1,2,0:T(8,128)S(1)}, u32[]{:S(2)}) copy-start(f32[3,256,128]{1,2,0:T(8,128)S(1)} %copy.68) | copy-start | bytes 1179652
  285.9 4.9 %collective-permute-start.1 = (f32[2,3,256]{2,0,1:T(2,128)S(1)}, f32[2,3,256]{2,0,1:T(2,128)S(1)}, u32[]{:S(2)}, u32[]{:S(2)}) collective-permute-start(f32[2,3,256]{2,0,1:T(2,128)S(1)} %slice.110), channel_id=1, source_target_pairs={{4,0},{8,4},{12,8},{16,12},{20,16},{24,20},{28,24},{32,28},{36,32}... | collective-permute-start | bytes 18440 | tf_op jit(solution)/shard_map/ppermute | solution.py:14
  290.8 6.4 %copy-start.1 = (bf16[256,4096]{0,1:T(8,128)(2,1)S(1)}, bf16[256,4096]{0,1:T(8,128)(2,1)}, u32[]{:S(2)}) copy-start(bf16[256,4096]{0,1:T(8,128)(2,1)} %all-gather.5.cloned.1.call-done) | copy-start | bytes 6291460
  296.0 3.1 copy-start.2
  296.0 54.9 %collective-permute-start.2 = (f32[128,4096]{1,0:T(8,128)S(1)}, f32[128,4096]{1,0:T(8,128)}, u32[]{:S(2)}, u32[]{:S(2)}) collective-permute-start(f32[128,4096]{1,0:T(8,128)S(1)} %convolution_bitcast_fusion), channel_id=1, source_target_pairs={{0,1},{1,0},{2,3},{3,2},{4,5},{5,4},{6,7},{7,6},{8,9},{9,8},{10,11... | collective-permute-start | bytes 6291464 | tf_op jit(solution)/shard_map/ppermute | solution.py:147
  353.4 49.2 %collective-permute-start.3 = (f32[128,4096]{1,0:T(8,128)S(1)}, f32[128,4096]{1,0:T(8,128)}, u32[]{:S(2)}, u32[]{:S(2)}) collective-permute-start(f32[128,4096]{1,0:T(8,128)S(1)} %add.156), channel_id=1, source_target_pairs={{0,2},{1,3},{2,0},{3,1},{4,6},{5,7},{6,4},{7,5},{8,10},{9,11},{10,... | collective-permute-start | bytes 6291464 | tf_op jit(solution)/shard_map/ppermute | solution.py:147
  356.2 46.4 %copy-start.8 = (f32[4096]{0:T(1024)S(1)}, f32[4096]{0:T(1024)}, u32[]{:S(2)}) copy-start(f32[4096]{0:T(1024)} %param.9) | copy-start | bytes 49156
  361.2 43.5 %copy-start.4 = (bf16[128,4096]{1,0:T(8,128)(2,1)S(1)}, bf16[128,4096]{1,0:T(8,128)(2,1)}, u32[]{:S(2)}) copy-start(bf16[128,4096]{1,0:T(8,128)(2,1)} %param.15) | copy-start | bytes 3145732
  361.2 43.5 %copy-start.11 = (f32[128]{0:T(128)S(1)}, f32[128]{0:T(128)}, u32[]{:S(2)}) copy-start(f32[128]{0:T(128)} %copy-done.10) | copy-start | bytes 1540
Sparse Core Ops, SparseCore 0:
  10.8 84.6 all-gather.2
  98.3 74.0 all-gather.4
  299.2 28.2 reduce-scatter.1
